TPU v7x, 768 devices: a whole 4x8x12 slice. The times are simulated.
768 devices in a mesh: segment: 8 (over x, core), field: 12 (over z), row: 8 (over y).
Axes of the slice: x: 4, y: 8, z: 12, core: 2. Of those that a mesh axis runs over, the one named last changes fastest.
Arguments:
- embeddings: bfloat16 [8, 1024, 192, 256], P('segment', 'row', 'field'), may hold values from -6 to 6
- compress: bfloat16 [8, 192, 8], P('segment'), may hold values from -1.5 to 1.5
- mixing: bfloat16 [8, 1536, 49152], P('segment', None, ('field', 'row')), may hold values from -0.15625 to 0.15625
- rescale_factor: float32 [8, 192, 256], P('segment', 'field'), may hold values from 0.5 to 1.5
- active_block_flags: int32 [12, 3], P('field'), may hold values from 1 to 3
Outputs:
- handed_on: bfloat16 [8, 1024, 192, 256], P('segment', 'row', 'field')
All inputs are finite; a program needn't handle non-finite values.
Results may differ from a plain program's by a relative error of at most 0.013.
Values may be sent and summed in bfloat16 or wider, within the bound.
No kernel may reach another device: no remote copies, remote signals or barrier semaphores. Data moves between devices by JAX's collectives and lax.ppermute only.
A program may use at most 128 MiB of HBM per device.

v0:
```python
import math

import jax
import jax.numpy as jnp
from jax import lax
from jax.sharding import PartitionSpec as P


def padded(array, sides, width):
    for axis, dim in sides:
        count, length = (lax.axis_size(axis), array.shape[dim])
        up = [(i, (i + 1) % count) for i in range(count)]
        down = [(j, i) for i, j in up]
        last = lax.slice_in_dim(array, length - width, length, axis=dim)
        initial = lax.slice_in_dim(array, 0, width, axis=dim)
        before = lax.ppermute(last, axis, up)
        after = lax.ppermute(initial, axis, down)
        array = jnp.concatenate([before, array, after], axis=dim)
    return array


def from_behind(array, axis, by):
    count = lax.axis_size(axis)
    return lax.ppermute(array, axis, [(i, (i + by) % count) for i in range(count)])


def squeeze_block(compress_rows, block_panel, block_index, field_dev):
    block_weights = lax.dynamic_slice_in_dim(compress_rows, block_index * field_dev, field_dev, 0)
    return jnp.einsum(
        "ak,rae->rke", block_weights, block_panel, preferred_element_type=jnp.float32
    ).astype(jnp.bfloat16)


def shards(embeddings, compress, mixing, rescale_factor, active_block_flags):
    own_panel = embeddings[0]
    device_rows, field_dev, feature_width = own_panel.shape
    owners = lax.axis_size("field")
    groups = lax.axis_size("row")
    myself = lax.axis_index("field")
    compress_rows = compress[0]
    rank_size = compress_rows.shape[1]
    beside_all = padded(own_panel[None], (("field", 0),), 1)
    reduced = jnp.stack(
        [
            squeeze_block(
                compress_rows,
                beside_all[offset_ordinal],
                (myself + offset_ordinal - 1 + owners) % owners,
                field_dev,
            )
            for offset_ordinal in range(3)
        ]
    )
    block_activity = active_block_flags[0].astype(jnp.float32)
    diagonal_block_products = jnp.einsum(
        "rae,drke->drak", own_panel, reduced, preferred_element_type=jnp.float32
    )
    pairwise_feature_product = (
        block_activity[0] * diagonal_block_products[0]
        + block_activity[1] * diagonal_block_products[1]
        + block_activity[2] * diagonal_block_products[2]
    )
    rank_rows = (
        (pairwise_feature_product * (1.0 / math.sqrt(feature_width)))
        .astype(jnp.bfloat16)
        .reshape(device_rows, field_dev * rank_size)
    )
    weights = mixing[0]
    block_span = field_dev * rank_size
    column_count = weights.shape[1]
    slabs = weights.reshape(owners, block_span, column_count)
    pieces = lax.all_gather(rank_rows[None], ("field", "row"), axis=0, tiled=True)
    member_count = pieces.shape[0]
    flat_index = jnp.arange(member_count, dtype=jnp.int32)
    owner_ids = flat_index // groups
    group_ids = flat_index % groups
    chosen = jnp.take(slabs, owner_ids, axis=0)
    contrib = jnp.einsum("mrc,mcd->mrd", pieces, chosen, preferred_element_type=jnp.float32)
    selector = (group_ids[:, None] == jnp.arange(groups, dtype=jnp.int32)[None, :]).astype(
        jnp.float32
    )
    placed = jnp.einsum("mg,mrd->grd", selector, contrib)
    projected = placed.reshape(groups * device_rows, column_count)
    fields_each = field_dev // groups
    local_mix = projected.astype(jnp.bfloat16).reshape(
        groups * device_rows, fields_each, feature_width
    )
    mixed_back = lax.all_to_all(local_mix, "row", split_axis=0, concat_axis=1, tiled=True)
    summed = own_panel.astype(jnp.float32) + mixed_back.astype(jnp.float32)
    mean_square = jnp.mean(summed * summed, axis=-1, keepdims=True)
    normed = (summed * lax.rsqrt(mean_square + 1e-06) * rescale_factor[0][None]).astype(
        jnp.bfloat16
    )
    handed = from_behind(normed, "segment", 1)
    return handed[None]


def solution(mesh):
    placed = (
        P("segment", "row", "field", None),
        P("segment", None, None),
        P("segment", None, ("field", "row")),
        P("segment", "field", None),
        P("field", None),
    )
    return jax.shard_map(
        shards,
        mesh=mesh,
        in_specs=placed,
        out_specs=P("segment", "row", "field", None),
        check_vma=False,
    )
```

profile of v0, /device:TPU:1, one launch (start us, length us, event | category | flops | bytes accessed | tf_op | source)
XLA Modules:
  0.0 262.2 jit_solution(15242613787255500433)
XLA Ops:
  6.5 4.9 %collective-permute-start = (bf16[1,128,16,256]{3,2,1,0:T(8,128)(2,1)}, bf16[1,128,16,256]{3,2,1,0:T(8,128)(2,1)}, u32[]{:S(2)}, u32[]{:S(2)}) collective-permute-start(bf16[1,128,16,256]{3,2,1,0:T(8,128)(2,1)} %param.5), channel_id=1, source_target_pairs={{0,8},{8,16},{16,24},{24,32},{32,40},{40,48},{48,56},{56,64},{64,7... | collective-permute-start | bytes 3145736 | tf_op jit(solution)/shard_map/ppermute | solution.py:16
  11.5 12.2 %collective-permute-start.1 = (bf16[1,128,16,256]{3,2,1,0:T(8,128)(2,1)}, bf16[1,128,16,256]{3,2,1,0:T(8,128)(2,1)}, u32[]{:S(2)}, u32[]{:S(2)}) collective-permute-start(bf16[1,128,16,256]{3,2,1,0:T(8,128)(2,1)} %param.5), channel_id=1, source_target_pairs={{8,0},{16,8},{24,16},{32,24},{40,32},{48,40},{56,48},{64,56},{72,6... | collective-permute-start | bytes 3145736 | tf_op jit(solution)/shard_map/ppermute | solution.py:17
  23.8 0.7 convert_element_type.57
  24.5 0.7 fusion.37
  25.1 1.7 fusion.12
  26.8 18.2 %collective-permute-done = bf16[1,128,16,256]{3,2,1,0:T(8,128)(2,1)} collective-permute-done((bf16[1,128,16,256]{3,2,1,0:T(8,128)(2,1)}, bf16[1,128,16,256]{3,2,1,0:T(8,128)(2,1)}, u32[]{:S(2)}, u32[]{:S(2)}) %collective-permute-start) | collective-permute-done | bytes 1048608 | tf_op jit(solution)/shard_map/ppermute | solution.py:16
  45.0 1.6 fusion.11
  46.6 0.0 collective-permute-done.1
  46.6 0.0 copy-done.3
  46.6 1.6 fusion.13
  48.2 1.7 fusion.6
  49.9 1.8 copy.38
  51.7 1.9 fusion.22
  53.7 0.7 copy.39
  54.4 0.0 all-gather.2.cloned.1.call-update
  54.5 6.8 %gather_fusion = bf16[96,128,512]{2,1,0:T(8,128)(2,1)} fusion(bf16[12,128,512]{2,1,0:T(8,128)(2,1)S(1)} %bitcast.68, s32[1024]{0:T(1024)S(1)} %pad_clamp_fusion), kind=kCustom, calls=%fused_computation | custom fusion | bytes 25166208 | tf_op jit(solution)/shard_map/jit(_take)/gather | solution.py:77
  61.3 109.7 %all-gather.2.cloned.1.call-done = bf16[96,128,128]{2,1,0:T(8,128)(2,1)} async-done(((bf16[1,128,128]{2,1,0:T(8,128)(2,1)}), bf16[96,128,128]{2,1,0:T(8,128)(2,1)}) %all-gather.2.cloned.1.call-update) | async-done | bytes 3145744 | tf_op jit(solution)/shard_map/all_gather | solution.py:72
  171.0 10.2 %fusion.2 = bf16[96,128,512]{2,1,0:T(8,128)(2,1)} fusion(bf16[96,128,128]{2,1,0:T(8,128)(2,1)} %all-gather.2.cloned.1.call-done, bf16[96,128,512]{2,1,0:T(8,128)(2,1)} %gather_fusion, pred[96]{0:T(512)(128)(4,1)S(1)} %compare_and_fusion), kind=kOutput, calls=%fused_computation.3 | convolution fusion | flops 1616904192 | bytes 28311648 | tf_op jit(solution)/shard_map/mrc,mcd->mrd/dot_general | solution.py:78
  181.2 17.9 %fusion.8 = bf16[8,128,512]{2,0,1:T(8,128)(2,1)S(1)} fusion(bf16[96,128,512]{2,1,0:T(8,128)(2,1)} %fusion.2, s32[96]{0:T(128)S(1)} %and_select_fusion.2), kind=kOutput, calls=%fused_computation.14 | convolution fusion | flops 100664064 | bytes 13631872 | tf_op jit(solution)/shard_map/mg,mrd->grd/dot_general | solution.py:82
  199.1 1.3 copy.49
  200.4 2.1 reshape.151
  202.5 27.6 %all_to_all.4 = bf16[1024,2,256]{2,1,0:T(2,128)(2,1)S(1)} all-to-all(bf16[1024,2,256]{2,1,0:T(2,128)(2,1)} %reshape.151), channel_id=1, replica_groups=mesh['segment'=8,'field'=12,'row'=8] {'row'}, dimensions={0} | all-to-all | bytes 2097152 | tf_op jit(solution)/shard_map/all_to_all | solution.py:88
  230.2 0.1 copy.43
  230.3 0.2 convert_bitcast_fusion
  230.5 0.1 copy.44
  230.7 0.0 copy-start.2
  230.7 0.4 multiply_reduce_fusion
  231.1 0.3 copy-done.2
  231.4 0.6 multiply_convert_fusion
  232.0 10.0 %collective-permute-start.2 = (bf16[128,16,256]{2,0,1:T(8,128)(2,1)S(1)}, bf16[128,16,256]{2,0,1:T(8,128)(2,1)S(1)}, u32[]{:S(2)}, u32[]{:S(2)}) collective-permute-start(bf16[128,16,256]{2,0,1:T(8,128)(2,1)S(1)} %multiply_convert_fusion), channel_id=1, source_target_pairs={{0,96},{96,192},{192,288},{288,384},{384,480},{480,576},{576,672},... | collective-permute-start | bytes 3145736 | tf_op jit(solution)/shard_map/ppermute | solution.py:24
  242.0 11.7 %collective-permute-done.2 = bf16[128,16,256]{2,0,1:T(8,128)(2,1)S(1)} collective-permute-done((bf16[128,16,256]{2,0,1:T(8,128)(2,1)S(1)}, bf16[128,16,256]{2,0,1:T(8,128)(2,1)S(1)}, u32[]{:S(2)}, u32[]{:S(2)}) %collective-permute-start.2) | collective-permute-done | bytes 1048608 | tf_op jit(solution)/shard_map/ppermute | solution.py:24
  253.8 1.6 copy.45
  (11 shorter events, 0.0 us)
Async XLA Ops:
  6.5 47.9 %copy-start = (bf16[1,1536,512]{2,1,0:T(8,128)(2,1)S(1)}, bf16[1,1536,512]{2,1,0:T(8,128)(2,1)}, u32[]{:S(2)}) copy-start(bf16[1,1536,512]{2,1,0:T(8,128)(2,1)} %param.7) | copy-start | bytes 4718596
  6.5 40.0 %copy-start.3 = (bf16[1,192,8]{1,2,0:T(8,128)(2,1)S(1)}, bf16[1,192,8]{1,2,0:T(8,128)(2,1)}, u32[]{:S(2)}) copy-start(bf16[1,192,8]{1,2,0:T(8,128)(2,1)} %param.6) | copy-start | bytes 9220
  6.5 164.5 %all-gather.2.cloned.1.call-start = ((), (), s32[]{:S(2)}) async-start(), calls=%async_computation.1 | async-start | bytes 3178496 | tf_op jit(solution)/shard_map/all_gather | solution.py:72
  6.5 38.4 %collective-permute-start = (bf16[1,128,16,256]{3,2,1,0:T(8,128)(2,1)}, bf16[1,128,16,256]{3,2,1,0:T(8,128)(2,1)}, u32[]{:S(2)}, u32[]{:S(2)}) collective-permute-start(bf16[1,128,16,256]{3,2,1,0:T(8,128)(2,1)} %param.5), channel_id=1, source_target_pairs={{0,8},{8,16},{16,24},{24,32},{32,40},{40,48},{48,56},{56,64},{64,7... | collective-permute-start | bytes 3145736 | tf_op jit(solution)/shard_map/ppermute | solution.py:16
  11.5 35.1 %collective-permute-start.1 = (bf16[1,128,16,256]{3,2,1,0:T(8,128)(2,1)}, bf16[1,128,16,256]{3,2,1,0:T(8,128)(2,1)}, u32[]{:S(2)}, u32[]{:S(2)}) collective-permute-start(bf16[1,128,16,256]{3,2,1,0:T(8,128)(2,1)} %param.5), channel_id=1, source_target_pairs={{8,0},{16,8},{24,16},{32,24},{40,32},{48,40},{56,48},{64,56},{72,6... | collective-permute-start | bytes 3145736 | tf_op jit(solution)/shard_map/ppermute | solution.py:17
  25.1 23.1 %copy-start.1 = (bf16[1,128,16,256]{3,2,1,0:T(8,128)(2,1)S(1)}, bf16[1,128,16,256]{3,2,1,0:T(8,128)(2,1)}, u32[]{:S(2)}) copy-start(bf16[1,128,16,256]{3,2,1,0:T(8,128)(2,1)} %param.5) | copy-start | bytes 3145732
  230.7 0.7 copy-start.2
  232.0 21.8 %collective-permute-start.2 = (bf16[128,16,256]{2,0,1:T(8,128)(2,1)S(1)}, bf16[128,16,256]{2,0,1:T(8,128)(2,1)S(1)}, u32[]{:S(2)}, u32[]{:S(2)}) collective-permute-start(bf16[128,16,256]{2,0,1:T(8,128)(2,1)S(1)} %multiply_convert_fusion), channel_id=1, source_target_pairs={{0,96},{96,192},{192,288},{288,384},{384,480},{480,576},{576,672},... | collective-permute-start | bytes 3145736 | tf_op jit(solution)/shard_map/ppermute | solution.py:24
Sparse Core Ops, SparseCore 0:
  54.5 116.4 all-gather.1
where the time goes:
time: 263 us; the launch traced here: 262 us
  waiting for transfers between devices  140 us (53%)
  matrix products  34.7 us (13%)
  blocking collectives  27.6 us (10%)
  starting transfers between devices  27.2 us (10%)
  local copies, waits for them, and re-layouts  15.6 us (6%)
  between operations  13.6 us (5%)
  other arithmetic  3.86 us (1%)
    all_gather x1, waiting for transfers between devices, shards(): lax.all_gather(rank_rows[None], ('field', 'row'), axis=0, tiled=True)  110 us
    all_to_all x1, blocking collectives, shards(): lax.all_to_all(local_mix, 'row', split_axis=0, concat_axis=1, tiled=True)  27.6 us
    ppermute x1, waiting for transfers between devices, padded(): before = lax.ppermute(last, axis, up)  18.2 us
    dot_general x1, matrix products, shards(): placed = jnp.einsum('mg,mrd->grd', selector, contrib)  17.9 us
    ppermute x1, starting transfers between devices, padded(): after = lax.ppermute(initial, axis, down)  12.2 us
    ppermute x1, waiting for transfers between devices, from_behind(): lax.ppermute(array, axis, [(i, (i + by) % count) for i in range(count)])  11.7 us
    dot_general x1, matrix products, shards(): jnp.einsum('mrc,mcd->mrd', pieces, chosen, preferred_element_type=jnp.flo...  10.2 us
    ppermute x1, starting transfers between devices, from_behind(): lax.ppermute(array, axis, [(i, (i + by) % count) for i in range(count)])  10 us
  transfers between devices with their start and end apart: 4, of which 3 were waited for; matrix products, arithmetic and copies ran while one was open for 4% of the time, Pallas kernels for 0%

commit v1 on v0

v1 whole, which is shorter than its diff:
```python
import math

import jax
import jax.numpy as jnp
from jax import lax
from jax.sharding import PartitionSpec as P


def shift(array, axis, by):
    count = lax.axis_size(axis)
    return lax.ppermute(array, axis, [(i, (i + by) % count) for i in range(count)])


def shards(embeddings, compress, mixing, rescale_factor, active_block_flags):
    own_panel = embeddings[0]
    device_rows, field_dev, feature_width = own_panel.shape
    owners = lax.axis_size("field")
    myself = lax.axis_index("field")
    compress_rows = compress[0]
    rank_size = compress_rows.shape[1]
    block_weights = lax.dynamic_slice_in_dim(compress_rows, myself * field_dev, field_dev, 0)
    reduced = jnp.einsum(
        "ak,rae->rke", block_weights, own_panel, preferred_element_type=jnp.float32
    ).astype(jnp.bfloat16)
    partners = jnp.concatenate(
        [shift(reduced, "field", 1), reduced, shift(reduced, "field", -1)], axis=1
    )
    products = jnp.einsum(
        "rae,rke->rak", own_panel, partners, preferred_element_type=jnp.float32
    ).reshape(device_rows, field_dev, 3, rank_size)
    block_activity = active_block_flags[0].astype(jnp.float32)
    pairwise_feature_product = jnp.einsum("rajk,j->rak", products, block_activity)
    rank_rows = (
        (pairwise_feature_product * (1.0 / math.sqrt(feature_width)))
        .astype(jnp.bfloat16)
        .reshape(device_rows, field_dev * rank_size)
    )
    pieces = lax.all_gather(rank_rows, "field", axis=0)
    pieces = lax.all_gather(pieces, "row", axis=0)
    weights = mixing[0]
    column_count = weights.shape[1]
    slabs = weights.reshape(owners, field_dev * rank_size, column_count)
    projected = jnp.einsum(
        "yfrc,fcd->yrd", pieces, slabs, preferred_element_type=jnp.float32
    )
    groups = pieces.shape[0]
    fields_each = field_dev // groups
    local_mix = projected.astype(jnp.bfloat16).reshape(
        groups * device_rows, fields_each, feature_width
    )
    mixed_back = lax.all_to_all(local_mix, "row", split_axis=0, concat_axis=1, tiled=True)
    summed = own_panel.astype(jnp.float32) + mixed_back.astype(jnp.float32)
    mean_square = jnp.mean(summed * summed, axis=-1, keepdims=True)
    normed = (summed * lax.rsqrt(mean_square + 1e-06) * rescale_factor[0][None]).astype(
        jnp.bfloat16
    )
    handed = shift(normed, "segment", 1)
    return handed[None]


def solution(mesh):
    placed = (
        P("segment", "row", "field", None),
        P("segment", None, None),
        P("segment", None, ("field", "row")),
        P("segment", "field", None),
        P("field", None),
    )
    return jax.shard_map(
        shards,
        mesh=mesh,
        in_specs=placed,
        out_specs=P("segment", "row", "field", None),
        check_vma=False,
    )
```

time: 263 us -> 184 us (0.70)
  waiting for transfers between devices: 140 us -> 77.3 us
  matrix products: 34.7 us -> 8.32 us
  blocking collectives: 27.6 us -> 49.7 us
  local copies, waits for them, and re-layouts: 15.6 us -> 6.79 us
  starting transfers between devices: 27.2 us -> 20.8 us
    all_gather x1, waiting for transfers between devices: 110 us -> 51.8 us  [shards(): pieces = lax.all_gather(pieces, 'row', axis=0)]
    dot_general x6 -> x4, matrix products: 34.7 us -> 8.32 us  [the longest x1 4.65 us: shards(): jnp.einsum('yfrc,fcd->yrd', pieces, slabs, preferred_element_type=jnp.flo...]
    all_gather x0 -> x1, blocking collectives: none -> 18.2 us  [shards(): pieces = lax.all_gather(rank_rows, 'field', axis=0)]
    gather x1 -> x0, local copies, waits for them, and re-layouts: 6.84 us -> none  [shards(): chosen = jnp.take(slabs, owner_ids, axis=0)]
    ppermute x3, starting transfers between devices: 27.2 us -> 20.8 us  [shift(): lax.ppermute(array, axis, [(i, (i + by) % count) for i in range(count)])]
    ppermute x3, waiting for transfers between devices: 29.9 us -> 25.4 us  [shift(): lax.ppermute(array, axis, [(i, (i + by) % count) for i in range(count)])]
    all_to_all x1, blocking collectives: 27.6 us -> 31.5 us  [shards(): lax.all_to_all(local_mix, 'row', split_axis=0, concat_axis=1, tiled=True)]
    convert_element_type x1, local copies, waits for them, and re-layouts: 0.14 us -> 3.75 us  [shards(): summed = own_panel.astype(jnp.float32) + mixed_back.astype(jnp.float32)]
  transfers between devices with their start and end apart: 4 -> 4, of which waited for: 3 -> 4; matrix products, arithmetic and copies ran while one was open for 4% -> 0% of each run, Pallas kernels for 0% -> 0%
where the time goes in v1:
time: 184 us; the launch traced here: 183 us
  waiting for transfers between devices  77.3 us (42%)
  blocking collectives  49.7 us (27%)
  starting transfers between devices  20.8 us (11%)
  between operations  13.5 us (7%)
  matrix products  8.32 us (5%)
  local copies, waits for them, and re-layouts  6.79 us (4%)
  other arithmetic  6.48 us (4%)
    all_gather x1, waiting for transfers between devices, shards(): pieces = lax.all_gather(pieces, 'row', axis=0)  51.8 us
    all_to_all x1, blocking collectives, shards(): lax.all_to_all(local_mix, 'row', split_axis=0, concat_axis=1, tiled=True)  31.5 us
    ppermute x3, waiting for transfers between devices, shift(): lax.ppermute(array, axis, [(i, (i + by) % count) for i in range(count)])  25.4 us
    ppermute x3, starting transfers between devices, shift(): lax.ppermute(array, axis, [(i, (i + by) % count) for i in range(count)])  20.8 us
    all_gather x1, blocking collectives, shards(): pieces = lax.all_gather(rank_rows, 'field', axis=0)  18.2 us
    dot_general x1, matrix products, shards(): jnp.einsum('yfrc,fcd->yrd', pieces, slabs, preferred_element_type=jnp.flo...  4.65 us
    convert_element_type x1, local copies, waits for them, and re-layouts, shards(): summed = own_panel.astype(jnp.float32) + mixed_back.astype(jnp.float32)  3.75 us
  transfers between devices with their start and end apart: 4, of which 4 were waited for; matrix products, arithmetic and copies ran while one was open for 0% of the time, Pallas kernels for 0%

profile of v1, /device:TPU:1, one launch (start us, length us, event | category | flops | bytes accessed | tf_op | source)
XLA Modules:
  0.0 182.9 jit_solution(7920904282851580481)
XLA Ops:
  6.5 0.0 copy-start
  6.5 0.0 all-gather.3.cloned.1.call-start
  6.5 1.7 fusion.9
  8.3 0.0 copy-start.3
  8.3 15.1 %collective-permute-start.1 = (bf16[128,8,256]{2,1,0:T(8,128)(2,1)S(1)}, bf16[128,8,256]{2,1,0:T(8,128)(2,1)S(1)}, u32[]{:S(2)}, u32[]{:S(2)}) collective-permute-start(bf16[128,8,256]{2,1,0:T(8,128)(2,1)S(1)} %fusion.9), channel_id=1, source_target_pairs={{0,88},{8,0},{16,8},{24,16},{32,24},{40,32},{48,40},{56,48},{64,56... | collective-permute-start | bytes 1572872 | tf_op jit(solution)/shard_map/ppermute | solution.py:11
  23.4 1.9 %collective-permute-start = (bf16[128,8,256]{2,1,0:T(8,128)(2,1)S(1)}, bf16[128,8,256]{2,1,0:T(8,128)(2,1)S(1)}, u32[]{:S(2)}, u32[]{:S(2)}) collective-permute-start(bf16[128,8,256]{2,1,0:T(8,128)(2,1)S(1)} %fusion.9), channel_id=1, source_target_pairs={{0,8},{8,16},{16,24},{24,32},{32,40},{40,48},{48,56},{56,64},{64,7... | collective-permute-start | bytes 1572872 | tf_op jit(solution)/shard_map/ppermute | solution.py:11
  25.3 8.7 %collective-permute-done.1 = bf16[128,8,256]{2,1,0:T(8,128)(2,1)S(1)} collective-permute-done((bf16[128,8,256]{2,1,0:T(8,128)(2,1)S(1)}, bf16[128,8,256]{2,1,0:T(8,128)(2,1)S(1)}, u32[]{:S(2)}, u32[]{:S(2)}) %collective-permute-start.1) | collective-permute-done | bytes 524320 | tf_op jit(solution)/shard_map/ppermute | solution.py:11
  34.0 5.0 %collective-permute-done = bf16[128,8,256]{2,1,0:T(8,128)(2,1)S(1)} collective-permute-done((bf16[128,8,256]{2,1,0:T(8,128)(2,1)S(1)}, bf16[128,8,256]{2,1,0:T(8,128)(2,1)S(1)}, u32[]{:S(2)}, u32[]{:S(2)}) %collective-permute-start) | collective-permute-done | bytes 524320 | tf_op jit(solution)/shard_map/ppermute | solution.py:11
  39.0 1.8 fusion.6
  40.8 0.4 copy.17
  41.2 0.0 copy-done.3
  41.2 0.2 fusion.12
  41.5 0.1 copy.18
  41.6 18.2 %all_gather.9 = bf16[12,128,128]{2,1,0:T(8,128)(2,1)} all-gather(bf16[1,128,128]{2,1,0:T(8,128)(2,1)S(1)} %copy.18), channel_id=1, replica_groups=mesh['segment'=8,'field'=12,'row'=8] {'field'}, dimensions={0}, use_global_device_ids=true | all-gather | bytes 425984 | tf_op jit(solution)/shard_map/all_gather | solution.py:38
  59.8 0.0 all-gather.3.cloned.1.call-update
  59.8 51.8 %all-gather.3.cloned.1.call-done = bf16[96,128,128]{2,1,0:T(8,128)(2,1)} async-done(((bf16[12,128,128]{2,1,0:T(8,128)(2,1)}), bf16[96,128,128]{2,1,0:T(8,128)(2,1)}) %all-gather.3.cloned.1.call-update) | async-done | bytes 3145744 | tf_op jit(solution)/shard_map/all_gather | solution.py:39
  111.6 0.0 copy-done
  111.6 4.6 %bitcast_convert_fusion = bf16[8,128,512]{2,1,0:T(8,128)(2,1)} fusion(bf16[8,12,128,128]{3,2,1,0:T(8,128)(2,1)} %bitcast.48, bf16[12,128,512,1]{2,1,0,3:T(8,128)(2,1)S(1)} %bitcast.42), kind=kOutput, calls=%fused_computation | convolution fusion | flops 1611137024 | bytes 5767168 | tf_op jit(solution)/shard_map/yfrc,fcd->yrd/dot_general | solution.py:43
  116.3 1.3 reshape.21
  117.6 31.5 %all_to_all.4 = bf16[1024,2,256]{2,1,0:T(2,128)(2,1)S(1)} all-to-all(bf16[1024,2,256]{2,1,0:T(2,128)(2,1)S(1)} %reshape.21), channel_id=1, replica_groups=mesh['segment'=8,'field'=12,'row'=8] {'row'}, dimensions={0} | all-to-all | bytes 2097152 | tf_op jit(solution)/shard_map/all_to_all | solution.py:51
  149.2 2.5 %copy_bitcast_fusion = f32[128,8,2,256]{3,2,1,0:T(2,128)} fusion(bf16[8,128,2,256]{3,2,1,0:T(2,128)(2,1)S(1)} %bitcast.43), kind=kLoop, calls=%fused_computation.1 | loop fusion | flops 524288 | bytes 3145728 | tf_op jit(solution)/shard_map/convert_element_type | solution.py:52
  151.7 0.0 copy-start.1
  151.7 3.7 %reshape.22 = f32[128,16,256]{2,1,0:T(8,128)} reshape(f32[128,8,2,256]{3,2,1,0:T(2,128)} %copy_bitcast_fusion) | data formatting | bytes 4194304 | tf_op jit(solution)/shard_map/convert_element_type | solution.py:52
  155.5 0.0 copy-done.1
  155.5 2.0 %multiply_reduce_fusion = f32[128,16]{1,0:T(8,128)S(1)} fusion(f32[128,16,256]{2,1,0:T(8,128)} %reshape.22, bf16[1,128,16,256]{3,2,1,0:T(8,128)(2,1)S(1)} %copy-done.1), kind=kLoop, calls=%fused_computation.3 | loop fusion | flops 2095104 | bytes 3153920 | tf_op jit(solution)/shard_map/reduce_sum | solution.py:53
  157.4 0.1 copy.20
  157.5 0.1 copy.21
  157.6 0.0 copy-done.2
  157.6 2.0 %multiply_convert_fusion = bf16[128,16,256]{2,1,0:T(8,128)(2,1)S(1)} fusion(f32[128,16,256]{2,1,0:T(8,128)} %reshape.22, bf16[1,128,16,256]{3,2,1,0:T(8,128)(2,1)S(1)} %copy-done.1, f32[16,256]{1,0:T(8,128)S(1)} %bitcast.47, f32[128,16]{1,0:T(8,128)S(1)} %copy.21), kind=kLoop, calls=%fused_computation.2 | loop fusion | flops 2621440 | bytes 4218880 | tf_op jit(solution)/shard_map/convert_element_type | solution.py:54
  159.6 3.8 %collective-permute-start.2 = (bf16[128,16,256]{2,1,0:T(8,128)(2,1)S(1)}, bf16[128,16,256]{2,1,0:T(8,128)(2,1)S(1)}, u32[]{:S(2)}, u32[]{:S(2)}) collective-permute-start(bf16[128,16,256]{2,1,0:T(8,128)(2,1)S(1)} %multiply_convert_fusion), channel_id=1, source_target_pairs={{0,96},{96,192},{192,288},{288,384},{384,480},{480,576},{576,672},... | collective-permute-start | bytes 3145736 | tf_op jit(solution)/shard_map/ppermute | solution.py:11
  163.3 11.7 %collective-permute-done.2 = bf16[128,16,256]{2,1,0:T(8,128)(2,1)S(1)} collective-permute-done((bf16[128,16,256]{2,1,0:T(8,128)(2,1)S(1)}, bf16[128,16,256]{2,1,0:T(8,128)(2,1)S(1)}, u32[]{:S(2)}, u32[]{:S(2)}) %collective-permute-start.2) | collective-permute-done | bytes 1048608 | tf_op jit(solution)/shard_map/ppermute | solution.py:11
  175.1 1.0 copy.30
  (3 shorter events, 0.0 us)
Async XLA Ops:
  6.5 105.1 %copy-start = (bf16[1,1536,512]{2,1,0:T(8,128)(2,1)S(1)}, bf16[1,1536,512]{2,1,0:T(8,128)(2,1)}, u32[]{:S(2)}) copy-start(bf16[1,1536,512]{2,1,0:T(8,128)(2,1)} %param.7) | copy-start | bytes 4718596
  6.5 105.1 %all-gather.3.cloned.1.call-start = ((), (), s32[]{:S(2)}) async-start(), calls=%async_computation.1 | async-start | bytes 3538944 | tf_op jit(solution)/shard_map/all_gather | solution.py:39
  8.3 33.0 %copy-start.3 = (s32[1,3]{1,0:T(1,128)S(1)}, s32[1,3]{1,0:T(1,128)}, u32[]{:S(2)}) copy-start(s32[1,3]{1,0:T(1,128)} %param.9) | copy-start | bytes 40
  8.3 25.7 %collective-permute-start.1 = (bf16[128,8,256]{2,1,0:T(8,128)(2,1)S(1)}, bf16[128,8,256]{2,1,0:T(8,128)(2,1)S(1)}, u32[]{:S(2)}, u32[]{:S(2)}) collective-permute-start(bf16[128,8,256]{2,1,0:T(8,128)(2,1)S(1)} %fusion.9), channel_id=1, source_target_pairs={{0,88},{8,0},{16,8},{24,16},{32,24},{40,32},{48,40},{56,48},{64,56... | collective-permute-start | bytes 1572872 | tf_op jit(solution)/shard_map/ppermute | solution.py:11
  23.4 15.6 %collective-permute-start = (bf16[128,8,256]{2,1,0:T(8,128)(2,1)S(1)}, bf16[128,8,256]{2,1,0:T(8,128)(2,1)S(1)}, u32[]{:S(2)}, u32[]{:S(2)}) collective-permute-start(bf16[128,8,256]{2,1,0:T(8,128)(2,1)S(1)} %fusion.9), channel_id=1, source_target_pairs={{0,8},{8,16},{16,24},{24,32},{32,40},{40,48},{48,56},{56,64},{64,7... | collective-permute-start | bytes 1572872 | tf_op jit(solution)/shard_map/ppermute | solution.py:11
  151.7 3.8 %copy-start.1 = (bf16[1,128,16,256]{3,2,1,0:T(8,128)(2,1)S(1)}, bf16[1,128,16,256]{3,2,1,0:T(8,128)(2,1)}, u32[]{:S(2)}) copy-start(bf16[1,128,16,256]{3,2,1,0:T(8,128)(2,1)} %param.5) | copy-start | bytes 3145732
  155.5 2.1 %copy-start.2 = (f32[1,16,256]{2,1,0:T(8,128)S(1)}, f32[1,16,256]{2,1,0:T(8,128)}, u32[]{:S(2)}) copy-start(f32[1,16,256]{2,1,0:T(8,128)} %param.8) | copy-start | bytes 49156
  159.6 15.5 %collective-permute-start.2 = (bf16[128,16,256]{2,1,0:T(8,128)(2,1)S(1)}, bf16[128,16,256]{2,1,0:T(8,128)(2,1)S(1)}, u32[]{:S(2)}, u32[]{:S(2)}) collective-permute-start(bf16[128,16,256]{2,1,0:T(8,128)(2,1)S(1)} %multiply_convert_fusion), channel_id=1, source_target_pairs={{0,96},{96,192},{192,288},{288,384},{384,480},{480,576},{576,672},... | collective-permute-start | bytes 3145736 | tf_op jit(solution)/shard_map/ppermute | solution.py:11
Sparse Core Ops, SparseCore 0:
  59.9 51.6 all-gather.2
